TPU v7x, 128 devices: a whole 4x4x4 slice. The times are simulated.
128 devices in a mesh: seq: 32 (over z, y, core), head: 4 (over x).
Axes of the slice: x: 4, y: 4, z: 4, core: 2. Of those that a mesh axis runs over, the one named last changes fastest.
Arguments:
- queries: bfloat16 [32768, 4096], P(('seq', 'head')), may hold values from -6 to 6
- key_rows: bfloat16 [32768, 4096], P(('seq', 'head')), may hold values from -6 to 6
- value_rows: bfloat16 [32768, 4096], P(('seq', 'head')), may hold values from -6 to 6
- decay_rates: float32 [32], replicated, as said below
- norm_gain: float32 [4096], replicated, may hold values from 0.5 to 1.5
Outputs:
- attended: bfloat16 [32768, 4096], P(('seq', 'head'))
Inputs may be any that keep to these rules, and one draw needn't show every extreme that they name: `decay_rates`: one positive rate per head.
All inputs are finite; a program needn't handle non-finite values.
Results may differ from a plain program's by a relative error of at most 0.003.
Values may be sent and summed in bfloat16 or wider, within the bound.
No kernel may reach another device: no remote copies, remote signals or barrier semaphores. Data moves between devices by JAX's collectives and lax.ppermute only.
A program may use at most 512 MiB of HBM per device.

v0:
```python
import jax
import jax.numpy as jnp
from jax import lax
from jax.sharding import PartitionSpec as P

HEADS = 32
HEAD_DIM = 128
BLOCK = 256


def carried_in(shard, axis, combine, identity):
    size, here = (lax.axis_size(axis), lax.axis_index(axis))
    everything = jax.tree.map(lambda part: lax.all_gather(part, axis), shard)
    start = jax.tree.map(
        lambda part, zero: jnp.broadcast_to(jnp.asarray(zero, part.dtype), part.shape),
        shard,
        identity,
    )

    def hop(k, before):
        reached = k < here
        new = combine(before, jax.tree.map(lambda part: part[k], everything))
        return jax.tree.map(lambda a, b: jnp.where(reached, a, b), new, before)

    return lax.fori_loop(0, size, hop, start)


def block_chain(queries, key_rows, value_rows, rates, block):
    tokens, heads, width = queries.shape
    count = tokens // block
    q_blocks = queries.reshape(count, block, heads, width)
    k_blocks = key_rows.reshape(count, block, heads, width)
    v_blocks = value_rows.reshape(count, block, heads, width)
    positions = jnp.arange(block, dtype=jnp.float32)
    offsets = positions[:, None] - positions[None, :]
    within = jnp.where(
        offsets[None] >= 0.0, jnp.exp(-rates[:, None, None] * jnp.maximum(offsets, 0.0)[None]), 0.0
    )
    q_decay = jnp.exp(-rates[None, :] * (positions[:, None] + 1.0))[:, :, None]
    k_decay = jnp.exp(-rates[None, :] * (block - 1.0 - positions[:, None]))[:, :, None]
    carry_decay = jnp.exp(-rates * block)[:, None, None]

    def advance(state, items):
        q_part, k_part, v_part = items
        scores = jnp.einsum("ihe,jhe->hij", q_part, k_part, preferred_element_type=jnp.float32)
        weights = (scores * within).astype(jnp.bfloat16)
        intra = jnp.einsum("hij,jhe->ihe", weights, v_part, preferred_element_type=jnp.float32)
        inter = jnp.einsum(
            "ihe,hef->ihf",
            q_part.astype(jnp.float32) * q_decay,
            state,
            precision=lax.Precision.HIGHEST,
        )
        added = jnp.einsum(
            "jhe,jhf->hef",
            k_part.astype(jnp.float32) * k_decay,
            v_part.astype(jnp.float32),
            precision=lax.Precision.HIGHEST,
        )
        return (carry_decay * state + added, intra + inter)

    start = jnp.zeros((heads, width, width), jnp.float32)
    state, outputs = lax.scan(advance, start, (q_blocks, k_blocks, v_blocks))
    return (outputs.reshape(tokens, heads, width), state)


def combine_states(earlier, later):
    return (earlier[0] * later[0], later[0][:, None, None] * earlier[1] + later[1])


def add_incoming(partial_value, queries, rates, incoming):
    span = queries.shape[0]
    positions = jnp.arange(span, dtype=jnp.float32)
    q_decay = jnp.exp(-rates[None, :] * (positions[:, None] + 1.0))[:, :, None]
    return partial_value + jnp.einsum(
        "ihe,hef->ihf",
        queries.astype(jnp.float32) * q_decay,
        incoming,
        precision=lax.Precision.HIGHEST,
    )


def normalize(total, gains):
    mean_square = jnp.mean(total * total, axis=-1, keepdims=True)
    normed = (total * lax.rsqrt(mean_square + 1e-06) * gains).astype(jnp.bfloat16)
    return normed.reshape(total.shape[0], total.shape[1] * total.shape[2])


def body(queries, key_rows, value_rows, decay_rates, norm_gain):
    group_heads = HEADS // lax.axis_size("head")
    first_head = lax.axis_index("head") * group_heads
    rates = lax.dynamic_slice_in_dim(decay_rates, first_head, group_heads)
    gains = lax.dynamic_slice_in_dim(
        norm_gain, first_head * HEAD_DIM, group_heads * HEAD_DIM
    ).reshape(group_heads, HEAD_DIM)
    q_group, k_group, v_group = (
        lax.all_to_all(queries, "head", split_axis=1, concat_axis=0, tiled=True),
        lax.all_to_all(key_rows, "head", split_axis=1, concat_axis=0, tiled=True),
        lax.all_to_all(value_rows, "head", split_axis=1, concat_axis=0, tiled=True),
    )
    span = q_group.shape[0]
    shaped = (span, group_heads, HEAD_DIM)
    q_group = q_group.reshape(shaped)
    partial_value, local_state = block_chain(
        q_group, k_group.reshape(shaped), v_group.reshape(shaped), rates, BLOCK
    )
    span_decay = jnp.exp(-rates * span)
    identity = (jnp.ones_like(span_decay), jnp.zeros_like(local_state))
    _, incoming = carried_in((span_decay, local_state), "seq", combine_states, identity)
    total = add_incoming(partial_value, q_group, rates, incoming)
    normed = normalize(total, gains)
    return lax.all_to_all(normed, "head", split_axis=0, concat_axis=1, tiled=True)


def solution(mesh):
    return jax.shard_map(
        body,
        mesh=mesh,
        in_specs=(
            P(("seq", "head"), None),
            P(("seq", "head"), None),
            P(("seq", "head"), None),
            P(),
            P(),
        ),
        out_specs=P(("seq", "head"), None),
        check_vma=False,
    )
```

profile of v0, /device:TPU:0, one launch (start us, length us, event | category | flops | bytes accessed | tf_op | source)
XLA Modules:
  0.0 421.3 jit_solution(12384549919905973251)
XLA Ops:
  6.5 4.1 copy.57
  10.6 4.6 %all-to-all-start.2 = ((bf16[256,4,1024]{0,2,1:T(8,128)(2,1)}), bf16[256,4,1024]{0,2,1:T(8,128)(2,1)}, u32[]{:S(2)}, u32[]{:S(2)}) async-start(bf16[256,4,1024]{0,2,1:T(8,128)(2,1)} %bitcast.7), calls=%async_computation.2 | async-start | bytes 4194304 | tf_op jit(solution)/shard_map/all_to_all | solution.py:97
  15.3 2.5 copy.55
  17.7 24.0 %all-to-all-done.2 = bf16[256,4,1024]{0,2,1:T(8,128)(2,1)} async-done(((bf16[256,4,1024]{0,2,1:T(8,128)(2,1)}), bf16[256,4,1024]{0,2,1:T(8,128)(2,1)}, u32[]{:S(2)}, u32[]{:S(2)}) %all-to-all-start.2) | async-done | bytes 2097184 | tf_op jit(solution)/shard_map/all_to_all | solution.py:97
  41.8 4.6 %all-to-all-start = ((bf16[256,4,1024]{0,2,1:T(8,128)(2,1)}), bf16[256,4,1024]{0,2,1:T(8,128)(2,1)}, u32[]{:S(2)}, u32[]{:S(2)}) async-start(bf16[256,4,1024]{0,2,1:T(8,128)(2,1)} %bitcast.1), calls=%async_computation | async-start | bytes 4194304 | tf_op jit(solution)/shard_map/all_to_all | solution.py:98
  46.4 2.5 copy.56
  48.9 23.1 %all-to-all-done = bf16[256,4,1024]{0,2,1:T(8,128)(2,1)} async-done(((bf16[256,4,1024]{0,2,1:T(8,128)(2,1)}), bf16[256,4,1024]{0,2,1:T(8,128)(2,1)}, u32[]{:S(2)}, u32[]{:S(2)}) %all-to-all-start) | async-done | bytes 2097184 | tf_op jit(solution)/shard_map/all_to_all | solution.py:98
  72.0 4.6 %all-to-all-start.1 = ((bf16[256,4,1024]{0,2,1:T(8,128)(2,1)}), bf16[256,4,1024]{0,2,1:T(8,128)(2,1)}, u32[]{:S(2)}, u32[]{:S(2)}) async-start(bf16[256,4,1024]{0,2,1:T(8,128)(2,1)} %bitcast.4), calls=%async_computation.1 | async-start | bytes 4194304 | tf_op jit(solution)/shard_map/all_to_all | solution.py:99
  78.3 23.0 %all-to-all-done.1 = bf16[256,4,1024]{0,2,1:T(8,128)(2,1)} async-done(((bf16[256,4,1024]{0,2,1:T(8,128)(2,1)}), bf16[256,4,1024]{0,2,1:T(8,128)(2,1)}, u32[]{:S(2)}, u32[]{:S(2)}) %all-to-all-start.1) | async-done | bytes 2097184 | tf_op jit(solution)/shard_map/all_to_all | solution.py:99
  101.2 139.2 %while.30 = (s32[]{:T(128)}, f32[8,128,128]{2,1,0:T(8,128)S(1)}, f32[4,256,8,128]{1,0,3,2:T(4,128)}, f32[8,1,1]{0,2,1:T(1,128)S(1)}, bf16[4,256,8,128]{1,3,2,0:T...) while((s32[]{:T(128)}, f32[8,128,128]{2,1,0:T(8,128)S(1)}, ...), condition=%wide.region_1.2_spmd.clone.clone.clone, body=%wide.region_0.1_spmd.clone.clone.clone.sunk | while | flops 1077678080 | bytes 16617720 | solution.py:63
  101.2 1.3 constant_dynamic-slice_fusion.7
  102.9 1.4 convolution_bitcast_fusion.2
  104.3 3.3 fusion.63
  107.6 2.3 copy.90
  109.9 23.4 %dynamic_update_slice.8 = f32[4,256,8,128]{1,0,3,2:T(4,128)} dynamic-update-slice(f32[4,256,8,128]{1,0,3,2:T(4,128)} %get-tuple-element.510, f32[1,256,8,128]{1,0,3,2:T(1,128)S(1)} %copy.90, s32[]{:T(128)} %get-tuple-element.508, s32[]{:T(128)} %constant.58.clone.1..sunk.1, s32[]{:T(128)} %constant.58.clone.1..sunk.1, s32[]{:T(128)} %constant.58.clone.1..sunk.1) | dynamic-update-slice | bytes 2097156 | tf_op jit(solution)/shard_map/while/body/jit(dynamic_update_index_in_dim)/dynamic_update_slice | solution.py:63
  133.6 2.4 convolution_add_fusion.2
  136.0 1.3 constant_dynamic-slice_fusion.7
  137.7 1.4 convolution_bitcast_fusion.2
  139.1 3.3 fusion.63
  142.4 2.3 copy.90
  144.7 23.4 %dynamic_update_slice.8 = f32[4,256,8,128]{1,0,3,2:T(4,128)} dynamic-update-slice(f32[4,256,8,128]{1,0,3,2:T(4,128)} %get-tuple-element.510, f32[1,256,8,128]{1,0,3,2:T(1,128)S(1)} %copy.90, s32[]{:T(128)} %get-tuple-element.508, s32[]{:T(128)} %constant.58.clone.1..sunk.1, s32[]{:T(128)} %constant.58.clone.1..sunk.1, s32[]{:T(128)} %constant.58.clone.1..sunk.1) | dynamic-update-slice | bytes 2097156 | tf_op jit(solution)/shard_map/while/body/jit(dynamic_update_index_in_dim)/dynamic_update_slice | solution.py:63
  168.4 2.4 convolution_add_fusion.2
  170.9 1.3 constant_dynamic-slice_fusion.7
  172.5 1.4 convolution_bitcast_fusion.2
  173.9 3.3 fusion.63
  177.2 2.3 copy.90
  179.5 23.4 %dynamic_update_slice.8 = f32[4,256,8,128]{1,0,3,2:T(4,128)} dynamic-update-slice(f32[4,256,8,128]{1,0,3,2:T(4,128)} %get-tuple-element.510, f32[1,256,8,128]{1,0,3,2:T(1,128)S(1)} %copy.90, s32[]{:T(128)} %get-tuple-element.508, s32[]{:T(128)} %constant.58.clone.1..sunk.1, s32[]{:T(128)} %constant.58.clone.1..sunk.1, s32[]{:T(128)} %constant.58.clone.1..sunk.1) | dynamic-update-slice | bytes 2097156 | tf_op jit(solution)/shard_map/while/body/jit(dynamic_update_index_in_dim)/dynamic_update_slice | solution.py:63
  203.2 2.4 convolution_add_fusion.2
  205.7 1.3 constant_dynamic-slice_fusion.7
  207.3 1.4 convolution_bitcast_fusion.2
  208.7 3.3 fusion.63
  212.0 2.3 copy.90
  214.3 23.4 %dynamic_update_slice.8 = f32[4,256,8,128]{1,0,3,2:T(4,128)} dynamic-update-slice(f32[4,256,8,128]{1,0,3,2:T(4,128)} %get-tuple-element.510, f32[1,256,8,128]{1,0,3,2:T(1,128)S(1)} %copy.90, s32[]{:T(128)} %get-tuple-element.508, s32[]{:T(128)} %constant.58.clone.1..sunk.1, s32[]{:T(128)} %constant.58.clone.1..sunk.1, s32[]{:T(128)} %constant.58.clone.1..sunk.1) | dynamic-update-slice | bytes 2097156 | tf_op jit(solution)/shard_map/while/body/jit(dynamic_update_index_in_dim)/dynamic_update_slice | solution.py:63
  238.0 2.4 convolution_add_fusion.2
  241.3 67.8 %all-reduce = f32[256]{0:T(256)S(1)} all-reduce(f32[256]{0:T(256)S(1)} %get-tuple-element.372), channel_id=2, replica_groups=mesh['seq'=32,'head'=4] {'seq'}, use_global_device_ids=true, to_apply=%add | all-reduce | flops 256 | bytes 2048
  309.5 5.9 %reshape.189 = f32[1024,8,128]{0,2,1:T(8,128)} reshape(f32[4,256,8,128]{1,0,3,2:T(4,128)} %get-tuple-element.152) | data formatting | bytes 8388608 | tf_op jit(solution)/shard_map/reshape | solution.py:64
  315.4 3.9 bitcast_convert_fusion
  319.3 5.4 %copy.62 = f32[4,256,1024]{2,1,0:T(8,128)} copy(f32[4,256,1024]{1,2,0:T(8,128)} %bitcast_convert_fusion) | data formatting | bytes 8388608 | tf_op jit(solution)/shard_map/convert_element_type | solution.py:77
  324.7 3.2 copy.78
  327.9 3.9 bitcast_multiply_fusion
  331.8 38.8 %while.29 = (s32[]{:T(128)}, f32[8,128,128]{2,1,0:T(8,128)S(1)}, s32[]{:T(128)}, f32[32,8]{1,0:T(8,128)S(1)}, f32[32,8,128,128]{3,2,1,0:T(8,128)}, /*index=5*/s32[]{:T(128)}, s32[]{:T(128)}) while((s32[]{:T(128)}, f32[8,128,128]{2,1,0:T(8,128)S(1)}, s32[]{:T(128)}, f32[32,8]{1,0:T(8,128)S(1)}, f32[32,8,128,128]{3,2,1,0:T(8,128)}, ...), condition=%wide.region_3.4_spmd.clone, body=%wide.region_2.3_spmd.clone.sunk | while | flops 524292 | bytes 1573065 | solution.py:25
  331.8 1.2 fusion.55
  335.4 1.2 fusion.55
  370.6 8.1 %multiply_reduce_fusion = (f32[1024,8]{0,1:T(8,128)S(1)}, f32[1024,8,128]{0,2,1:T(8,128)S(1)}) fusion(f32[1024,8,128]{0,2,1:T(8,128)} %reshape.189, f32[8,128,128]{2,1,0:T(8,128)S(1)} %get-tuple-element.154, f32[1024,8,128]{2,1,0:T(8,128)} %bitcast_multiply_fusion), kind=kOutput, calls=%fused_computation.48 | convolution fusion | flops 1613750272 | bytes 13139968 | tf_op jit(solution)/shard_map/ihe,hef->ihf/dot_general | solution.py:75
  378.7 1.8 multiply_convert_fusion
  380.5 3.3 all_to_all.59
  384.1 27.5 %all_to_all.67 = bf16[4,256,1024]{1,2,0:T(8,128)(2,1)S(1)} all-to-all(bf16[4,256,1024]{1,2,0:T(8,128)(2,1)S(1)} %copy.66), channel_id=1, replica_groups=mesh['seq'=32,'head'=4] {'head'}, dimensions={0} | all-to-all | bytes 4194304 | tf_op jit(solution)/shard_map/all_to_all | solution.py:112
  411.6 2.8 copy.67
  (108 shorter events, 40.4 us)
Async XLA Ops:
  6.5 302.9 %copy-start = (f32[4096]{0:T(1024)S(1)}, f32[4096]{0:T(1024)}, u32[]{:S(2)}) copy-start(f32[4096]{0:T(1024)} %param.13) | copy-start | bytes 49156
  10.6 4.6 %copy-start.3 = (bf16[256,4096]{1,0:T(8,128)(2,1)S(1)}, bf16[256,4096]{1,0:T(8,128)(2,1)}, u32[]{:S(2)}) copy-start(bf16[256,4096]{1,0:T(8,128)(2,1)} %param.10) | copy-start | bytes 6291460
  10.6 31.1 %all-to-all-start.2 = ((bf16[256,4,1024]{0,2,1:T(8,128)(2,1)}), bf16[256,4,1024]{0,2,1:T(8,128)(2,1)}, u32[]{:S(2)}, u32[]{:S(2)}) async-start(bf16[256,4,1024]{0,2,1:T(8,128)(2,1)} %bitcast.7), calls=%async_computation.2 | async-start | bytes 4194304 | tf_op jit(solution)/shard_map/all_to_all | solution.py:97
  41.8 4.6 %copy-start.4 = (bf16[256,4096]{1,0:T(8,128)(2,1)S(1)}, bf16[256,4096]{1,0:T(8,128)(2,1)}, u32[]{:S(2)}) copy-start(bf16[256,4096]{1,0:T(8,128)(2,1)} %param.11) | copy-start | bytes 6291460
  41.8 30.2 %all-to-all-start = ((bf16[256,4,1024]{0,2,1:T(8,128)(2,1)}), bf16[256,4,1024]{0,2,1:T(8,128)(2,1)}, u32[]{:S(2)}, u32[]{:S(2)}) async-start(bf16[256,4,1024]{0,2,1:T(8,128)(2,1)} %bitcast.1), calls=%async_computation | async-start | bytes 4194304 | tf_op jit(solution)/shard_map/all_to_all | solution.py:98
  72.0 4.7 %copy-start.6 = (u32[128]{0:T(128)S(1)}, u32[128]{0:T(128)}, u32[]{:S(2)}) copy-start(u32[128]{0:T(128)} %constant.75) | copy-start | bytes 1540
  72.0 6.0 %copy-start.5 = (f32[32]{0:T(128)S(1)}, f32[32]{0:T(128)}, u32[]{:S(2)}) copy-start(f32[32]{0:T(128)} %param.12) | copy-start | bytes 388
  72.0 29.3 %all-to-all-start.1 = ((bf16[256,4,1024]{0,2,1:T(8,128)(2,1)}), bf16[256,4,1024]{0,2,1:T(8,128)(2,1)}, u32[]{:S(2)}, u32[]{:S(2)}) async-start(bf16[256,4,1024]{0,2,1:T(8,128)(2,1)} %bitcast.4), calls=%async_computation.1 | async-start | bytes 4194304 | tf_op jit(solution)/shard_map/all_to_all | solution.py:99
  76.6 255.2 %all-gather.4.cloned.1.call-start = ((), (), s32[]{:S(2)}) async-start(), calls=%async_computation.4 | async-start | bytes 17301504 | tf_op jit(solution)/shard_map/all_gather | solution.py:13
  240.5 0.8 copy-start.2
  411.6 2.9 copy-start.1
Sparse Core Ops, SparseCore 0:
  241.4 74.2 all-gather.3
where the time goes:
time: 426 us; the launch traced here: 421 us
  local copies, waits for them, and re-layouts  142 us (33%)
  blocking collectives  95.3 us (22%)
  waiting for transfers between devices  70.1 us (16%)
  other arithmetic  47.9 us (11%)
  matrix products  36.6 us (9%)
  between operations  14.3 us (3%)
  starting transfers between devices  13.8 us (3%)
    dynamic_update_slice x8, local copies, waits for them, and re-layouts, block_chain(): state, outputs = lax.scan(advance, start, (q_blocks, k_blocks, v_blocks))  103 us
    unnamed x1, blocking collectives  67.8 us
    select_n x32, other arithmetic, hop(): return jax.tree.map(lambda a, b: jnp.where(reached, a, b), new, before)  37.5 us
    all_to_all x1, blocking collectives, body(): lax.all_to_all(normed, 'head', split_axis=0, concat_axis=1, tiled=True)  27.5 us
    all_to_all x1, waiting for transfers between devices, body(): lax.all_to_all(queries, 'head', split_axis=1, concat_axis=0, tiled=True)  24 us
    all_to_all x1, waiting for transfers between devices, body(): lax.all_to_all(key_rows, 'head', split_axis=1, concat_axis=0, tiled=True)  23.1 us
    all_to_all x1, waiting for transfers between devices, body(): lax.all_to_all(value_rows, 'head', split_axis=1, concat_axis=0, tiled=True)  23 us
    unnamed x20, local copies, waits for them, and re-layouts  13.6 us
  transfers between devices with their start and end apart: 4, of which 3 were waited for; matrix products, arithmetic and copies ran while one was open for 7% of the time, Pallas kernels for 0%

commit v1 on v0

--- a/solution.py
+++ b/solution.py
@@ -6,6 +6,22 @@
 HEADS = 32
 HEAD_DIM = 128
 BLOCK = 256
+
+
+def exchange_in_pairs(x, axis, split, join):
+    ways, here = (lax.axis_size(axis), lax.axis_index(axis))
+    width = x.shape[split] // ways
+    lengths = list(x.shape)
+    lengths[split] = width
+    height = lengths[join]
+    lengths[join] = height * ways
+    full = jnp.zeros(lengths, x.dtype)
+    for mask in range(ways):
+        part = lax.dynamic_slice_in_dim(x, (here ^ mask) * width, width, axis=split)
+        if mask:
+            part = lax.ppermute(part, axis, [(d, d ^ mask) for d in range(ways)])
+        full = lax.dynamic_update_slice_in_dim(full, part, (here ^ mask) * height, axis=join)
+    return full
 
 
 def carried_in(shard, axis, combine, identity):
@@ -94,7 +110,7 @@
         norm_gain, first_head * HEAD_DIM, group_heads * HEAD_DIM
     ).reshape(group_heads, HEAD_DIM)
     q_group, k_group, v_group = (
-        lax.all_to_all(queries, "head", split_axis=1, concat_axis=0, tiled=True),
+        exchange_in_pairs(queries, "head", 1, 0),
         lax.all_to_all(key_rows, "head", split_axis=1, concat_axis=0, tiled=True),
         lax.all_to_all(value_rows, "head", split_axis=1, concat_axis=0, tiled=True),
     )

time: 426 us -> 407 us (0.955)
  waiting for transfers between devices: 70.1 us -> 57.2 us
  other arithmetic: 47.9 us -> 40.1 us
    ppermute x0 -> x3, waiting for transfers between devices: none -> 33.2 us  [exchange_in_pairs(): part = lax.ppermute(part, axis, [(d, d ^ mask) for d in range(ways)])]
    all_to_all x1 -> x0, waiting for transfers between devices: 24 us -> none  [body(): lax.all_to_all(queries, 'head', split_axis=1, concat_axis=0, tiled=True)]
    all_to_all x1, waiting for transfers between devices: 23 us -> 0.01 us  [body(): lax.all_to_all(value_rows, 'head', split_axis=1, concat_axis=0, tiled=True)]
    convert_element_type x1 -> x0, local copies, waits for them, and re-layouts: 5.41 us -> none  [add_incoming(): queries.astype(jnp.float32) * q_decay]
    dynamic_update_slice x0 -> x4, local copies, waits for them, and re-layouts: none -> 5.39 us  [exchange_in_pairs(): lax.dynamic_update_slice_in_dim(full, part, (here ^ mask) * height, axis=...]
    ppermute x0 -> x3, starting transfers between devices: none -> 4.94 us  [exchange_in_pairs(): part = lax.ppermute(part, axis, [(d, d ^ mask) for d in range(ways)])]
    dynamic_update_slice x8, local copies, waits for them, and re-layouts: 103 us -> 98 us  [block_chain(): state, outputs = lax.scan(advance, start, (q_blocks, k_blocks, v_blocks))]
    all_to_all x1 -> x0, starting transfers between devices: 4.63 us -> none  [body(): lax.all_to_all(queries, 'head', split_axis=1, concat_axis=0, tiled=True)]
  transfers between devices with their start and end apart: 4 -> 6, of which waited for: 3 -> 3; matrix products, arithmetic and copies ran while one was open for 7% -> 7% of each run, Pallas kernels for 0% -> 0%
where the time goes in v1:
time: 407 us; the launch traced here: 402 us
  local copies, waits for them, and re-layouts  141 us (35%)
  blocking collectives  98.9 us (24%)
  waiting for transfers between devices  57.2 us (14%)
  other arithmetic  40.1 us (10%)
  matrix products  35.1 us (9%)
  between operations  14.3 us (4%)
  starting transfers between devices  14.1 us (3%)
    dynamic_update_slice x8, local copies, waits for them, and re-layouts, block_chain(): state, outputs = lax.scan(advance, start, (q_blocks, k_blocks, v_blocks))  98 us
    unnamed x1, blocking collectives  68.4 us
    select_n x32, other arithmetic, hop(): return jax.tree.map(lambda a, b: jnp.where(reached, a, b), new, before)  37.5 us
    ppermute x3, waiting for transfers between devices, exchange_in_pairs(): part = lax.ppermute(part, axis, [(d, d ^ mask) for d in range(ways)])  33.2 us
    all_to_all x1, blocking collectives, body(): lax.all_to_all(normed, 'head', split_axis=0, concat_axis=1, tiled=True)  30.5 us
    all_to_all x1, waiting for transfers between devices, body(): lax.all_to_all(key_rows, 'head', split_axis=1, concat_axis=0, tiled=True)  24 us
    unnamed x21, local copies, waits for them, and re-layouts  13.6 us
    dot_general x4, matrix products, advance(): jnp.einsum('ihe,hef->ihf', q_part.astype(jnp.float32) * q_decay, state, p...  9.73 us
  transfers between devices with their start and end apart: 6, of which 3 were waited for; matrix products, arithmetic and copies ran while one was open for 7% of the time, Pallas kernels for 0%

profile of v1, /device:TPU:0, one launch (start us, length us, event | category | flops | bytes accessed | tf_op | source)
XLA Modules:
  0.0 402.1 jit_solution(15547987623077124326)
XLA Ops:
  6.5 4.1 %copy.46 = bf16[256,4096]{0,1:T(8,128)(2,1)} copy(bf16[256,4096]{1,0:T(8,128)(2,1)} %param.10) | data formatting | bytes 4194304 | tf_op args[1]
  10.6 4.6 %all-to-all-start = ((bf16[256,4,1024]{0,2,1:T(8,128)(2,1)}), bf16[256,4,1024]{0,2,1:T(8,128)(2,1)}, u32[]{:S(2)}, u32[]{:S(2)}) async-start(bf16[256,4,1024]{0,2,1:T(8,128)(2,1)} %bitcast.1), calls=%async_computation | async-start | bytes 4194304 | tf_op jit(solution)/shard_map/all_to_all | solution.py:114
  15.2 2.5 copy.47
  17.8 24.0 %all-to-all-done = bf16[256,4,1024]{0,2,1:T(8,128)(2,1)} async-done(((bf16[256,4,1024]{0,2,1:T(8,128)(2,1)}), bf16[256,4,1024]{0,2,1:T(8,128)(2,1)}, u32[]{:S(2)}, u32[]{:S(2)}) %all-to-all-start) | async-done | bytes 2097184 | tf_op jit(solution)/shard_map/all_to_all | solution.py:114
  41.8 4.6 %all-to-all-start.1 = ((bf16[256,4,1024]{0,2,1:T(8,128)(2,1)}), bf16[256,4,1024]{0,2,1:T(8,128)(2,1)}, u32[]{:S(2)}, u32[]{:S(2)}) async-start(bf16[256,4,1024]{0,2,1:T(8,128)(2,1)} %bitcast.4), calls=%async_computation.1 | async-start | bytes 4194304 | tf_op jit(solution)/shard_map/all_to_all | solution.py:115
  46.4 1.2 constant_dynamic-slice_fusion.3
  47.6 1.3 copy.73
  48.9 2.0 collective-permute-start
  50.9 1.2 copy.74
  52.1 2.8 collective-permute-start.1
  56.8 1.6 broadcast_in_dim.24
  59.5 24.5 %collective-permute-done = bf16[256,1024]{0,1:T(8,128)(2,1)} collective-permute-done((bf16[256,1024]{0,1:T(8,128)(2,1)S(1)}, bf16[256,1024]{0,1:T(8,128)(2,1)}, u32[]{:S(2)}, u32[]{:S(2)}) %collective-permute-start) | collective-permute-done | bytes 524320 | tf_op jit(solution)/shard_map/ppermute | solution.py:22
  84.0 1.9 constant_dynamic-update-slice_fusion.2
  85.9 8.7 %collective-permute-done.1 = bf16[256,1024]{0,1:T(8,128)(2,1)} collective-permute-done((bf16[256,1024]{0,1:T(8,128)(2,1)S(1)}, bf16[256,1024]{0,1:T(8,128)(2,1)}, u32[]{:S(2)}, u32[]{:S(2)}) %collective-permute-start.1) | collective-permute-done | bytes 524320 | tf_op jit(solution)/shard_map/ppermute | solution.py:22
  94.6 1.9 constant_dynamic-update-slice_fusion.1
  97.3 3.3 reshape.193
  100.6 2.6 copy.55
  103.2 132.2 %while.30 = (s32[]{:T(128)}, f32[8,128,128]{2,1,0:T(8,128)S(1)}, f32[4,256,8,128]{1,0,3,2:T(4,128)}, f32[8,1,1]{0,2,1:T(1,128)S(1)}, bf16[4,256,8,128]{1,3,2,0:T...) while((s32[]{:T(128)}, f32[8,128,128]{2,1,0:T(8,128)S(1)}, ...), condition=%wide.region_1.2_spmd.clone.clone.clone, body=%wide.region_0.1_spmd.clone.clone.clone.sunk | while | flops 1077678080 | bytes 14521080 | solution.py:79
  103.3 2.4 convolution_bitcast_fusion.2
  105.7 2.2 fusion.66
  109.1 23.4 %dynamic_update_slice.28 = f32[4,256,8,128]{1,0,3,2:T(4,128)} dynamic-update-slice(f32[4,256,8,128]{1,0,3,2:T(4,128)} %get-tuple-element.496, f32[1,256,8,128]{1,0,3,2:T(1,128)S(1)} %copy.80, s32[]{:T(128)} %get-tuple-element.494, s32[]{:T(128)} %constant.34.clone.1..sunk.1, s32[]{:T(128)} %constant.34.clone.1..sunk.1, s32[]{:T(128)} %constant.34.clone.1..sunk.1) | dynamic-update-slice | bytes 2097156 | tf_op jit(solution)/shard_map/while/body/jit(dynamic_update_index_in_dim)/dynamic_update_slice | solution.py:79
  133.8 2.4 convolution_add_fusion.2
  136.4 2.4 convolution_bitcast_fusion.2
  138.8 2.2 fusion.66
  142.1 23.4 %dynamic_update_slice.28 = f32[4,256,8,128]{1,0,3,2:T(4,128)} dynamic-update-slice(f32[4,256,8,128]{1,0,3,2:T(4,128)} %get-tuple-element.496, f32[1,256,8,128]{1,0,3,2:T(1,128)S(1)} %copy.80, s32[]{:T(128)} %get-tuple-element.494, s32[]{:T(128)} %constant.34.clone.1..sunk.1, s32[]{:T(128)} %constant.34.clone.1..sunk.1, s32[]{:T(128)} %constant.34.clone.1..sunk.1) | dynamic-update-slice | bytes 2097156 | tf_op jit(solution)/shard_map/while/body/jit(dynamic_update_index_in_dim)/dynamic_update_slice | solution.py:79
  166.9 2.4 convolution_add_fusion.2
  169.4 2.4 convolution_bitcast_fusion.2
  171.8 2.2 fusion.66
  175.2 23.4 %dynamic_update_slice.28 = f32[4,256,8,128]{1,0,3,2:T(4,128)} dynamic-update-slice(f32[4,256,8,128]{1,0,3,2:T(4,128)} %get-tuple-element.496, f32[1,256,8,128]{1,0,3,2:T(1,128)S(1)} %copy.80, s32[]{:T(128)} %get-tuple-element.494, s32[]{:T(128)} %constant.34.clone.1..sunk.1, s32[]{:T(128)} %constant.34.clone.1..sunk.1, s32[]{:T(128)} %constant.34.clone.1..sunk.1) | dynamic-update-slice | bytes 2097156 | tf_op jit(solution)/shard_map/while/body/jit(dynamic_update_index_in_dim)/dynamic_update_slice | solution.py:79
  199.9 2.4 convolution_add_fusion.2
  202.5 2.4 convolution_bitcast_fusion.2
  204.9 2.2 fusion.66
  208.2 23.4 %dynamic_update_slice.28 = f32[4,256,8,128]{1,0,3,2:T(4,128)} dynamic-update-slice(f32[4,256,8,128]{1,0,3,2:T(4,128)} %get-tuple-element.496, f32[1,256,8,128]{1,0,3,2:T(1,128)S(1)} %copy.80, s32[]{:T(128)} %get-tuple-element.494, s32[]{:T(128)} %constant.34.clone.1..sunk.1, s32[]{:T(128)} %constant.34.clone.1..sunk.1, s32[]{:T(128)} %constant.34.clone.1..sunk.1) | dynamic-update-slice | bytes 2097156 | tf_op jit(solution)/shard_map/while/body/jit(dynamic_update_index_in_dim)/dynamic_update_slice | solution.py:79
  233.0 2.4 convolution_add_fusion.2
  236.3 68.4 %all-reduce = f32[256]{0:T(256)S(1)} all-reduce(f32[256]{0:T(256)S(1)} %get-tuple-element.360), channel_id=2, replica_groups=mesh['seq'=32,'head'=4] {'seq'}, use_global_device_ids=true, to_apply=%add | all-reduce | flops 256 | bytes 2048
  304.9 5.8 %reshape.184 = f32[1024,8,128]{0,2,1:T(8,128)} reshape(f32[4,256,8,128]{1,0,3,2:T(4,128)} %get-tuple-element.152) | data formatting | bytes 8388608 | tf_op jit(solution)/shard_map/reshape | solution.py:80
  310.8 38.8 %while.29 = (s32[]{:T(128)}, f32[8,128,128]{2,1,0:T(8,128)S(1)}, s32[]{:T(128)}, f32[32,8]{1,0:T(8,128)S(1)}, f32[32,8,128,128]{3,2,1,0:T(8,128)}, /*index=5*/s32[]{:T(128)}, s32[]{:T(128)}) while((s32[]{:T(128)}, f32[8,128,128]{2,1,0:T(8,128)S(1)}, s32[]{:T(128)}, f32[32,8]{1,0:T(8,128)S(1)}, f32[32,8,128,128]{3,2,1,0:T(8,128)}, ...), condition=%wide.region_3.4_spmd.clone, body=%wide.region_2.3_spmd.clone.sunk | while | flops 524292 | bytes 1573065 | solution.py:41
  310.8 1.2 fusion.58
  314.4 1.2 fusion.58
  315.6 1.2 fusion.58
  316.8 1.2 fusion.58
  320.5 1.2 fusion.58
  321.7 1.2 fusion.58
  349.6 6.9 %multiply_reduce_fusion = (f32[1024,8]{0,1:T(8,128)S(1)}, f32[1024,8,128]{0,2,1:T(8,128)S(1)}) fusion(f32[1024,8,128]{0,2,1:T(8,128)} %reshape.184, f32[8,128,128]{2,1,0:T(8,128)S(1)} %get-tuple-element.154, bf16[1024,8,128]{0,2,1:T(8,128)(2,1)} %bitcast.27, f32[1024,8]{0,1:T(8,128)S(1)} %multiply_exponential_fusion), kind=kOutput, calls=%fused_computation.49 | convolution fusion | flops 1615847424 | bytes 11075584 | tf_op jit(solution)/shard_map/ihe,hef->ihf/dot_general | solution.py:91
  356.5 1.8 multiply_convert_fusion
  358.3 3.3 all_to_all.44
  361.9 30.5 %all_to_all.51 = bf16[4,256,1024]{1,2,0:T(8,128)(2,1)S(1)} all-to-all(bf16[4,256,1024]{1,2,0:T(8,128)(2,1)S(1)} %copy.59), channel_id=1, replica_groups=mesh['seq'=32,'head'=4] {'head'}, dimensions={0} | all-to-all | bytes 4194304 | tf_op jit(solution)/shard_map/all_to_all | solution.py:128
  392.4 2.8 copy.60
  (112 shorter events, 45.4 us)
Async XLA Ops:
  6.5 298.3 %copy-start = (f32[4096]{0:T(1024)S(1)}, f32[4096]{0:T(1024)}, u32[]{:S(2)}) copy-start(f32[4096]{0:T(1024)} %param.13) | copy-start | bytes 49156
  10.6 4.6 %copy-start.2 = (bf16[256,4096]{1,0:T(8,128)(2,1)S(1)}, bf16[256,4096]{1,0:T(8,128)(2,1)}, u32[]{:S(2)}) copy-start(bf16[256,4096]{1,0:T(8,128)(2,1)} %param.11) | copy-start | bytes 6291460
  10.6 31.1 %all-to-all-start = ((bf16[256,4,1024]{0,2,1:T(8,128)(2,1)}), bf16[256,4,1024]{0,2,1:T(8,128)(2,1)}, u32[]{:S(2)}, u32[]{:S(2)}) async-start(bf16[256,4,1024]{0,2,1:T(8,128)(2,1)} %bitcast.1), calls=%async_computation | async-start | bytes 4194304 | tf_op jit(solution)/shard_map/all_to_all | solution.py:114
  41.8 4.7 %copy-start.3 = (bf16[256,4096]{1,0:T(8,128)(2,1)S(1)}, bf16[256,4096]{1,0:T(8,128)(2,1)}, u32[]{:S(2)}) copy-start(bf16[256,4096]{1,0:T(8,128)(2,1)} %param.9) | copy-start | bytes 6291460
  41.8 61.5 %all-to-all-start.1 = ((bf16[256,4,1024]{0,2,1:T(8,128)(2,1)}), bf16[256,4,1024]{0,2,1:T(8,128)(2,1)}, u32[]{:S(2)}, u32[]{:S(2)}) async-start(bf16[256,4,1024]{0,2,1:T(8,128)(2,1)} %bitcast.4), calls=%async_computation.1 | async-start | bytes 4194304 | tf_op jit(solution)/shard_map/all_to_all | solution.py:115
  46.4 264.4 %all-gather.4.cloned.1.call-start = ((), (), s32[]{:S(2)}) async-start(), calls=%async_computation.3 | async-start | bytes 17301504 | tf_op jit(solution)/shard_map/all_gather | solution.py:29
  47.6 7.9 %copy-start.5 = (u32[128]{0:T(128)S(1)}, u32[128]{0:T(128)}, u32[]{:S(2)}) copy-start(u32[128]{0:T(128)} %constant.86) | copy-start | bytes 1540
  48.9 35.1 %collective-permute-start = (bf16[256,1024]{0,1:T(8,128)(2,1)S(1)}, bf16[256,1024]{0,1:T(8,128)(2,1)}, u32[]{:S(2)}, u32[]{:S(2)}) collective-permute-start(bf16[256,1024]{0,1:T(8,128)(2,1)S(1)} %copy.73), channel_id=1, source_target_pairs={{0,1},{1,0},{2,3},{3,2},{4,5},{5,4},{6,7},{7,6},{8,9},{9,8},{10,11... | collective-permute-start | bytes 1572872 | tf_op jit(solution)/shard_map/ppermute | solution.py:22
  52.1 42.4 %collective-permute-start.1 = (bf16[256,1024]{0,1:T(8,128)(2,1)S(1)}, bf16[256,1024]{0,1:T(8,128)(2,1)}, u32[]{:S(2)}, u32[]{:S(2)}) collective-permute-start(bf16[256,1024]{0,1:T(8,128)(2,1)S(1)} %copy.74), channel_id=1, source_target_pairs={{0,2},{1,3},{2,0},{3,1},{4,6},{5,7},{6,4},{7,5},{8,10},{9,11},{10,... | collective-permute-start | bytes 1572872 | tf_op jit(solution)/shard_map/ppermute | solution.py:22
  55.1 41.4 %collective-permute-start.2 = (bf16[256,1024]{0,1:T(8,128)(2,1)S(1)}, bf16[256,1024]{0,1:T(8,128)(2,1)S(1)}, u32[]{:S(2)}, u32[]{:S(2)}) collective-permute-start(bf16[256,1024]{0,1:T(8,128)(2,1)S(1)} %copy.75), channel_id=1, source_target_pairs={{0,3},{1,2},{2,1},{3,0},{4,7},{5,6},{6,5},{7,4},{8,11},{9,10},{10,... | collective-permute-start | bytes 1572872 | tf_op jit(solution)/shard_map/ppermute | solution.py:22
  55.3 4.0 %copy-start.4 = (f32[32]{0:T(128)S(1)}, f32[32]{0:T(128)}, u32[]{:S(2)}) copy-start(f32[32]{0:T(128)} %param.12) | copy-start | bytes 388
  235.4 0.8 copy-start.1
Sparse Core Ops, SparseCore 0:
  236.4 73.9 all-gather.3
